TPU v7x, 32 devices: a whole 2x2x4 slice. The times are simulated.
32 devices in a mesh: ctx: 8 (over z, x), head: 4 (over y, core).
Axes of the slice: x: 2, y: 2, z: 4, core: 2. Of those that a mesh axis runs over, the one named last changes fastest.
Arguments:
- queries: bfloat16 [4096, 4096], P('ctx', 'head'), may hold values from -6 to 6
- key_states: bfloat16 [4096, 4096], P('ctx', 'head'), may hold values from -6 to 6
- value_states: bfloat16 [4096, 4096], P('ctx', 'head'), may hold values from -6 to 6
- transition_vectors: bfloat16 [4096, 4096], P('ctx', 'head'), may hold values from -6 to 6
- beta_logit: float32 [4096, 32], P('ctx', 'head'), may hold values from -6 to 6
- document_ids: int32 [4096], P('ctx'), may hold values from 0 to 7, as said below
- out_weight: bfloat16 [4096, 4096], P('head'), may hold values from -0.09375 to 0.09375
Outputs:
- layer_out: bfloat16 [4096, 4096], P(('ctx', 'head'))
Inputs may be any that keep to these rules, and one draw needn't show every extreme that they name: `document_ids`: document ids never fall along the sequence; document 0 is the first 2304 tokens; the other documents have 1 or more tokens each and together fill the rest.
All inputs are finite; a program needn't handle non-finite values.
Results may differ from a plain program's by a relative error of at most 0.022.
Values may be sent and summed in bfloat16 or wider, within the bound.
No kernel may reach another device: no remote copies, remote signals or barrier semaphores. Data moves between devices by JAX's collectives and lax.ppermute only.
A program may use at most 128 MiB of HBM per device.

v0:
```python
import jax
import jax.numpy as jnp
from jax import lax
from jax.sharding import PartitionSpec as P

epsilon = 1e-06
masked_value = -1e30
highest = lax.Precision.HIGHEST


def shard_operators(query_block, key_block, vector_block, strength):
    block_rows = key_block.shape[0]
    head_width = key_block.shape[1]
    row_ids = jnp.arange(block_rows)
    strict = row_ids[:, None] > row_ids[None, :]
    causal = row_ids[:, None] >= row_ids[None, :]
    intersections = jnp.dot(vector_block, vector_block.T, precision=highest)
    unit_lower = jnp.where(strict, intersections * strength[None, :], 0.0) + jnp.eye(
        block_rows, dtype=jnp.float32
    )
    key_proj = jnp.where(strict, jnp.dot(vector_block, key_block.T, precision=highest), 0.0)
    solved = lax.linalg.triangular_solve(
        unit_lower,
        jnp.concatenate([key_proj, vector_block], axis=1),
        left_side=True,
        lower=True,
        unit_diagonal=True,
    )
    key_solve = solved[:, :block_rows]
    vector_solve = solved[:, block_rows:]
    weighted = strength[:, None] * vector_block
    keys_end = (key_block - jnp.dot(key_solve.T, weighted, precision=highest)).astype(jnp.bfloat16)
    transfer = jnp.eye(head_width, dtype=jnp.float32) - jnp.dot(
        vector_block.T, strength[:, None] * vector_solve, precision=highest
    )
    query_dots = jnp.where(causal, jnp.dot(query_block, vector_block.T, precision=highest), 0.0)
    scaled_dots = query_dots * strength[None, :]
    intra_scores = jnp.dot(query_block, key_block.T, precision=highest) - jnp.dot(
        scaled_dots, key_solve, precision=highest
    )
    rotated = query_block - jnp.dot(scaled_dots, vector_solve, precision=highest)
    return (intra_scores, keys_end, transfer, rotated)


def on_device(
    queries, key_states, value_states, transition_vectors, beta_logit, document_ids, out_weight
):
    block_rows = queries.shape[0]
    head_count = beta_logit.shape[1]
    head_width = queries.shape[1] // head_count
    score_scale = head_width ** (-0.5)

    def split_heads(flat):
        return jnp.transpose(flat.reshape(block_rows, head_count, head_width), (1, 0, 2))

    query_heads = split_heads(queries).astype(jnp.float32)
    key_heads = split_heads(key_states).astype(jnp.float32)
    value_heads = split_heads(value_states)
    vector_heads = split_heads(transition_vectors).astype(jnp.float32)
    unit_vectors = vector_heads / jnp.sqrt(
        jnp.sum(vector_heads * vector_heads, axis=2, keepdims=True) + epsilon
    )
    strength = 2.0 * jax.nn.sigmoid(beta_logit.T)
    intra_scores, keys_end, transfer, rotated = jax.vmap(shard_operators)(
        query_heads, key_heads, unit_vectors, strength
    )
    row_ids = jnp.arange(block_rows)
    causal = row_ids[:, None] >= row_ids[None, :]
    doc_float = (document_ids + 1).astype(jnp.float32)
    same_doc = doc_float[:, None] == doc_float[None, :]
    own_scores = jnp.where((causal & same_doc)[None], intra_scores * score_scale, masked_value)
    running_max = jnp.max(own_scores, axis=2)
    weights = jnp.exp(own_scores - running_max[..., None])
    running_sum = jnp.sum(weights, axis=2)
    accumulated = jnp.einsum(
        "hqk,hkd->hqd",
        weights.astype(jnp.bfloat16),
        value_heads,
        preferred_element_type=jnp.float32,
    )
    ctx_index = lax.axis_index("ctx")
    ctx_count = lax.axis_size("ctx")
    packed = jnp.stack([keys_end, value_heads])

    def attend(carried, key_pair, transfer_in, key_docs, is_live):
        turned, running_max, running_sum, accumulated = carried
        scores = jnp.einsum(
            "hqd,hkd->hqk",
            turned.astype(jnp.bfloat16),
            key_pair[0],
            preferred_element_type=jnp.float32,
        )
        allowed = (doc_float[:, None] == key_docs[None, :]) & is_live
        scores = jnp.where(allowed[None], scores * score_scale, masked_value)
        new_max = jnp.maximum(running_max, jnp.max(scores, axis=2))
        factor = jnp.exp(running_max - new_max)
        weights = jnp.exp(scores - new_max[..., None])
        running_sum = running_sum * factor + jnp.sum(weights, axis=2)
        accumulated = accumulated * factor[..., None] + jnp.einsum(
            "hqk,hkd->hqd",
            weights.astype(jnp.bfloat16),
            key_pair[1],
            preferred_element_type=jnp.float32,
        )
        turned = jnp.einsum("hqd,hde->hqe", turned, transfer_in, precision=highest)
        return (turned, new_max, running_sum, accumulated)

    def visit(carried, key_pair, transfer_in, key_docs, is_live):
        return attend(carried, key_pair, transfer_in, key_docs, is_live)

    carried = (rotated, running_max, running_sum, accumulated)
    every_pair = lax.all_gather(packed, "ctx", axis=2, tiled=True)
    every_transfer, every_doc = (
        lax.all_gather(transfer[None].astype(jnp.bfloat16), "ctx", axis=0, tiled=True).astype(
            jnp.float32
        ),
        lax.all_gather(doc_float.astype(jnp.bfloat16), "ctx", axis=0, tiled=True).astype(
            doc_float.dtype
        ),
    )

    def local_step(offset, inner):
        source = jnp.maximum(ctx_index - offset, 0)
        key_pair = lax.dynamic_slice_in_dim(every_pair, source * block_rows, block_rows, 2)
        transfer_in = lax.dynamic_index_in_dim(every_transfer, source, 0, keepdims=False)
        key_docs = lax.dynamic_slice_in_dim(every_doc, source * block_rows, block_rows, 0)
        return visit(inner, key_pair, transfer_in, key_docs, ctx_index - offset >= 0)

    carried = lax.fori_loop(1, ctx_count, local_step, carried)
    attended = (carried[3] / carried[2][..., None]).astype(jnp.bfloat16)
    token_rows = jnp.transpose(attended, (1, 0, 2)).reshape(block_rows, head_count * head_width)
    return lax.psum_scatter(
        jnp.dot(token_rows, out_weight, preferred_element_type=jnp.float32).astype(jnp.bfloat16),
        "head",
        scatter_dimension=0,
        tiled=True,
    )


def solution(mesh):
    return jax.shard_map(
        on_device,
        mesh=mesh,
        in_specs=(
            P("ctx", "head"),
            P("ctx", "head"),
            P("ctx", "head"),
            P("ctx", "head"),
            P("ctx", "head"),
            P("ctx"),
            P("head", None),
        ),
        out_specs=P(("ctx", "head"), None),
        check_vma=False,
    )
```

profile of v0, /device:TPU:0, one launch (start us, length us, event | category | flops | bytes accessed | tf_op | source)
XLA Modules:
  0.0 895.8 jit_solution(15207088580192670057)
XLA Ops:
  16.1 6.1 broadcast_select_fusion
  22.2 11.6 %select_add_fusion = f32[8,512,512]{1,2,0:T(8,128)} fusion(f32[512,512]{0,1:T(8,128)S(1)} %copy-done.22, f32[512,512]{0,1:T(8,128)S(1)} %copy-done.21, f32[8,512]{1,0:T(8,128)S(1)} %multiply_bitcast_fusion, pred[512,512]{0,1:T(8,128)(4,1)S(1)} %get-tuple-element.265, pred[512,512]{0,1:T(8,128)(4,1)S(1)} %copy-done.23, ...), kind=kOutput, calls=%fused_computation.42 | convolution fusion | flops 3231711232 | bytes 13123584 | tf_op jit(solution)/shard_map/vmap()/dot_general | solution.py:17
  33.8 17.5 %while.21 = (s32[]{:T(128)}, f32[8,512,512]{1,2,0:T(8,128)}, s32[4,2]{0,1:T(2,128)S(1)}, f32[4,8,128,128]{3,2,0,1:T(8,128)}, s32[]{:T(128)}) while((s32[]{:T(128)}, f32[8,512,512]{1,2,0:T(8,128)}, s32[4,2]{0,1:T(2,128)S(1)}, f32[4,8,128,128]{3,2,0,1:T(8,128)}, s32[]{:T(128)}) %tuple.58), condition=%wide.while_cond, body=%wide.while_body.sunk | while | flops 2 | bytes 3145845 | solution.py:22
  51.3 316.0 %custom-call.3 = f32[8,4,128,128]{2,3,1,0:T(8,128)} custom-call(f32[8,4,128,128]{3,2,1,0:T(8,128)} %bitcast.132), custom_call_target="InvertDiagBlocksLowerTriangular" | custom-call | tf_op jit(solution)/shard_map/vmap()/triangular_solve | solution.py:22
  367.4 4.7 fusion.52
  372.1 6.0 fusion.90
  378.1 4.7 fusion.56
  382.9 11.1 %fusion.33 = f32[8,128,640]{1,2,0:T(8,128)S(1)} fusion(f32[8,128,640]{2,1,0:T(8,128)S(1)} %fusion.56, f32[8,128,640]{2,1,0:T(8,128)S(1)} %fusion.52, f32[8,512,512]{1,2,0:T(8,128)} %get-tuple-element.434), kind=kOutput, calls=%fused_computation.54 | convolution fusion | flops 2014576640 | bytes 8912896 | tf_op jit(solution)/shard_map/vmap()/triangular_solve | solution.py:22
  394.0 3.0 fusion.49
  398.6 16.0 %fusion.21 = f32[8,128,640]{1,2,0:T(8,128)} fusion(f32[8,128,640]{2,1,0:T(8,128)S(1)} %fusion.49, f32[8,128,640]{2,1,0:T(8,128)S(1)} %fusion.56, f32[8,128,640]{2,1,0:T(8,128)S(1)} %fusion.52, f32[8,512,512]{1,2,0:T(8,128)} %get-tuple-element.434), kind=kOutput, calls=%fused_computation.43 | convolution fusion | flops 3023831040 | bytes 12058624 | tf_op jit(solution)/shard_map/vmap()/triangular_solve | solution.py:22
  414.6 3.3 copy.108
  417.9 3.3 copy.107
  421.2 3.2 copy.106
  424.4 5.2 fusion.59
  432.5 2.9 fusion.76
  438.4 10.1 %fusion.70 = bf16[1,8,512,128]{3,2,1,0:T(8,128)(2,1)S(1)} fusion(f32[8,512,128]{1,2,0:T(8,128)S(1)} %broadcast_divide_fusion, f32[8,128,640]{1,2,0:T(8,128)} %copy-done.8, f32[8,128,640]{1,2,0:T(8,128)} %copy.108, f32[8,128,640]{1,2,0:T(8,128)} %copy.107, f32[8,128,640]{1,2,0:T(8,128)} %copy.106, bf16[512,8,128]{2,0,1:T(8,128)(2,1)} %copy-done.14, ...), kind=kOutput, calls=%fused_computation.90 | convolution fusion | flops 3229614080 | bytes 14696448 | tf_op jit(solution)/shard_map/vmap()/dot_general | solution.py:32
  454.7 3.6 fusion.84
  458.3 3.3 copy-done.3
  461.6 15.8 %convert_subtract_fusion = f32[8,512,128]{2,1,0:T(8,128)} fusion(f32[8,512,128]{1,2,0:T(8,128)S(1)} %copy-done.7, f32[8,512,512]{2,1,0:T(8,128)S(1)} %fusion.84, f32[8,512]{1,0:T(8,128)S(1)} %multiply_bitcast_fusion, pred[512,512]{0,1:T(8,128)(4,1)S(1)} %iota_compare_fusion.4, bf16[512,8,128]{2,0,1:T(8,128)(2,1)S(1)} %copy.81), kind=kOutput, calls=%fused_computation.88 | convolution fusion | flops 3226468352 | bytes 13910016 | tf_op jit(solution)/shard_map/vmap()/dot_general | solution.py:41
  479.3 28.1 %all-gather.1 = bf16[8,1,512]{2,1,0:T(2,128)(2,1)S(1)} all-gather(bf16[1,1,512]{2,1,0:T(2,128)(2,1)S(1)} %reshape.148), channel_id=1, replica_groups=mesh['ctx'=8,'head'=4] {'ctx'}, dimensions={0}, use_global_device_ids=true | all-gather | bytes 9216 | tf_op jit(solution)/shard_map/all_gather | solution.py:117
  507.6 17.9 %fusion.29 = f32[8,512,512]{1,2,0:T(8,128)S(1)} fusion(f32[8,512,512]{2,1,0:T(8,128)} %copy-done.3, f32[8,512]{1,0:T(8,128)S(1)} %multiply_bitcast_fusion, pred[512,512]{0,1:T(8,128)(4,1)S(1)} %iota_compare_fusion.4, f32[8,128,640]{1,2,0:T(8,128)} %copy-done.8, f32[8,128,640]{1,2,0:T(8,128)} %copy.108, f32[8,128,640]{1,2,0:T(8,128)} %copy.107, ...), kind=kOutput, calls=%fused_computation.51 | convolution fusion | flops 12895387648 | bytes 27541504 | tf_op jit(solution)/shard_map/vmap()/dot_general | solution.py:38
  528.7 3.1 fusion.37
  531.7 4.1 convert.4
  535.9 180.1 %all-gather.5.cloned.1.call-done = bf16[2,8,4096,128]{3,2,1,0:T(8,128)(2,1)} async-done(((bf16[2,8,512,128]{3,2,1,0:T(8,128)(2,1)}), bf16[2,8,4096,128]{3,2,1,0:T(8,128)(2,1)}) %all-gather.5.cloned.1.call-update) | async-done | bytes 16777232 | tf_op jit(solution)/shard_map/all_gather | solution.py:112
  715.9 118.4 %while.20 = (s32[]{:T(128)}, f32[8,512,128]{1,2,0:T(8,128)S(1)}, f32[8,512]{1,0:T(8,128)S(1)}, f32[8,512]{1,0:T(8,128)S(1)}, f32[8,512,128]{2,1,0:T(8,128)}, /*i...) while((s32[]{:T(128)}, f32[8,512,128]{1,2,0:T(8,128)S(1)}, ...), condition=%wide.region_6.7_spmd, body=%wide.region_3.6_spmd.sunk | while | flops 1904222208 | bytes 77340952 | solution.py:129
  716.6 2.8 fusion.125
  719.4 3.4 convolution_bitcast_fusion.2
  724.6 8.4 multiply_add_fusion.5
  733.5 2.8 fusion.125
  736.3 3.4 convolution_bitcast_fusion.2
  741.5 8.4 multiply_add_fusion.5
  750.4 2.8 fusion.125
  753.2 3.4 convolution_bitcast_fusion.2
  758.4 8.4 multiply_add_fusion.5
  767.3 2.8 fusion.125
  770.1 3.4 convolution_bitcast_fusion.2
  775.3 8.4 multiply_add_fusion.5
  784.2 2.8 fusion.125
  786.9 3.4 convolution_bitcast_fusion.2
  792.1 8.4 multiply_add_fusion.5
  801.0 2.8 fusion.125
  803.8 3.4 convolution_bitcast_fusion.2
  809.0 8.4 multiply_add_fusion.5
  817.9 2.8 fusion.125
  820.7 3.4 convolution_bitcast_fusion.2
  825.9 8.4 multiply_add_fusion.5
  836.5 9.5 %convolution_convert_fusion = bf16[512,4096]{1,0:T(8,128)(2,1)} fusion(bf16[512,1024]{0,1:T(8,128)(2,1)S(1)} %bitcast.130, bf16[1024,4096]{1,0:T(8,128)(2,1)} %param.15), kind=kOutput, calls=%fused_computation.53 | convolution fusion | flops 4297064448 | bytes 13631488 | tf_op jit(solution)/shard_map/dot_general | solution.py:133
  846.1 42.9 %reduce-scatter.2.cloned.1.call-done = bf16[128,4096]{1,0:T(8,128)(2,1)} async-done(((bf16[512,4096]{1,0:T(8,128)(2,1)}), bf16[128,4096]{1,0:T(8,128)(2,1)}) %reduce-scatter.2.cloned.1.call-update) | async-done | bytes 1048592 | tf_op jit(solution)/shard_map/reduce_scatter | solution.py:132
  (174 shorter events, 63.8 us)
Async XLA Ops:
  6.5 2.6 copy-start.17
  6.5 525.2 %all-gather.7.cloned.1.call-start = ((), (), s32[]{:S(2)}) async-start(), calls=%async_computation.3 | async-start | bytes 2359296 | tf_op jit(solution)/shard_map/all_gather | solution.py:114
  9.7 1.4 copy-start.5
  11.0 2.0 copy-start.18
  13.0 3.0 copy-start.24
  16.0 6.2 copy-start.14
  16.0 6.1 copy-start.21
  16.0 6.1 copy-start.22
  16.1 6.1 copy-start.23
  367.3 10.7 %copy-start.16 = (f32[8,4,128,128]{2,3,1,0:T(8,128)S(1)}, f32[8,4,128,128]{2,3,1,0:T(8,128)}, u32[]{:S(2)}) copy-start(f32[8,4,128,128]{2,3,1,0:T(8,128)} %custom-call.3) | copy-start | bytes 6291460
  372.1 24.9 %copy-start.1 = (f32[8,128,640]{2,1,0:T(8,128)}, f32[8,128,640]{2,1,0:T(8,128)S(1)}, u32[]{:S(2)}) copy-start(f32[8,128,640]{2,1,0:T(8,128)S(1)} %fusion.52) | copy-start | bytes 7864324
  372.1 21.9 %slice-start = ((s8[8388608]{0:T(1024)(128)(4,1)}), s8[4194304]{0:T(1024)(128)(4,1)S(1)}, s32[]{:S(2)}) async-start(s8[8388608]{0:T(1024)(128)(4,1)} %bitcast.123), calls=%async_computation.4 | async-start | bytes 8388608
  378.1 15.9 %slice-start.1 = ((s8[8388608]{0:T(1024)(128)(4,1)}), s8[4194304]{0:T(1024)(128)(4,1)S(1)}, s32[]{:S(2)}) async-start(s8[8388608]{0:T(1024)(128)(4,1)} %bitcast.123), calls=%async_computation.5 | async-start | bytes 8388608
  382.8 14.1 %copy-start.2 = (f32[8,128,640]{2,1,0:T(8,128)}, f32[8,128,640]{2,1,0:T(8,128)S(1)}, u32[]{:S(2)}) copy-start(f32[8,128,640]{2,1,0:T(8,128)S(1)} %fusion.56) | copy-start | bytes 7864324
  397.0 1.6 copy-start.4
  424.4 5.2 copy-start.9
  424.4 5.2 copy-start.10
  424.4 5.2 copy-start.11
  429.7 1.4 copy-start.8
  431.1 1.4 copy-start.6
  432.5 3.0 copy-start.19
  435.4 280.5 %all-gather.5.cloned.1.call-start = ((), (), s32[]{:S(2)}) async-start(), calls=%async_computation.1 | async-start | bytes 18874368 | tf_op jit(solution)/shard_map/all_gather | solution.py:112
  438.4 10.1 %copy-start.12 = (bf16[512,8,128]{2,0,1:T(8,128)(2,1)}, bf16[512,8,128]{2,0,1:T(8,128)(2,1)S(1)}, u32[]{:S(2)}) copy-start(bf16[512,8,128]{2,0,1:T(8,128)(2,1)S(1)} %copy.114) | copy-start | bytes 3145732
  450.0 1.2 copy-start.20
  450.0 438.9 %reduce-scatter.2.cloned.1.call-start = ((), (), s32[]{:S(2)}) async-start(), calls=%async_computation.2 | async-start | bytes 5242880 | tf_op jit(solution)/shard_map/reduce_scatter | solution.py:132
  454.7 6.9 copy-start.7
  458.3 3.3 copy-start.3
  477.3 1.9 copy-start.25
  507.6 17.9 %copy-start.15 = (bf16[512,8,128]{2,0,1:T(8,128)(2,1)S(1)}, bf16[512,8,128]{2,0,1:T(8,128)(2,1)}, u32[]{:S(2)}) copy-start(bf16[512,8,128]{2,0,1:T(8,128)(2,1)} %copy-done.14) | copy-start | bytes 3145732
  527.4 1.2 copy-start.13
  719.4 5.2 copy-start
  736.3 5.2 copy-start
  753.2 5.2 copy-start
  770.0 5.2 copy-start
  786.9 5.2 copy-start
  803.8 5.2 copy-start
  820.7 5.2 copy-start
Sparse Core Ops, SparseCore 0:
  435.5 51.9 all-gather.6
  489.7 226.1 all-gather.4
  846.2 42.7 reduce-scatter.1
where the time goes:
time: 905 us; the launch traced here: 896 us
  other arithmetic  343 us (38%)
  matrix products  235 us (26%)
  waiting for transfers between devices  223 us (25%)
  local copies, waits for them, and re-layouts  52.5 us (6%)
  blocking collectives  28.1 us (3%)
  between operations  14 us (2%)
    another operation x3, other arithmetic, shard_operators(): lax.linalg.triangular_solve(unit_lower, jnp.concatenate([key_proj, vector...  316 us
    all_gather x1, waiting for transfers between devices, on_device(): every_pair = lax.all_gather(packed, 'ctx', axis=2, tiled=True)  180 us
    dot_general x7, matrix products, attend(): jnp.einsum('hqk,hkd->hqd', weights.astype(jnp.bfloat16), key_pair[1], pre...  58.8 us
    another operation x7, matrix products, shard_operators(): lax.linalg.triangular_solve(unit_lower, jnp.concatenate([key_proj, vector...  50.7 us
    reduce_scatter x1, waiting for transfers between devices, on_device(): lax.psum_scatter(jnp.dot(token_rows, out_weight, preferred_element_type=j...  42.9 us
    all_gather x1, blocking collectives, on_device(): lax.all_gather(doc_float.astype(jnp.bfloat16), 'ctx', axis=0, tiled=True)  28.1 us
    dot_general x7, matrix products, attend(): turned = jnp.einsum('hqd,hde->hqe', turned, transfer_in, precision=highest)  23.7 us
    dot_general x7, matrix products, attend(): jnp.einsum('hqd,hkd->hqk', turned.astype(jnp.bfloat16), key_pair[0], pref...  19.3 us
  transfers between devices with their start and end apart: 3, of which 2 were waited for; matrix products, arithmetic and copies ran while one was open for 8% of the time, Pallas kernels for 0%

commit v1 on v0

--- a/solution.py
+++ b/solution.py
@@ -6,6 +6,16 @@
 epsilon = 1e-06
 masked_value = -1e30
 highest = lax.Precision.HIGHEST
+
+
+def pass_along(x, mesh_axis, along):
+    devices = lax.axis_size(mesh_axis)
+    held, shards = (x, [x])
+    for _ in range(devices - 1):
+        held = lax.ppermute(held, mesh_axis, [(i, (i + 1) % devices) for i in range(devices)])
+        shards.insert(0, held)
+    flat = jnp.concatenate(shards, axis=along)
+    return jnp.roll(flat, (lax.axis_index(mesh_axis) + 1) * x.shape[along], axis=along)
 
 
 def shard_operators(query_block, key_block, vector_block, strength):
@@ -109,7 +119,7 @@
         return attend(carried, key_pair, transfer_in, key_docs, is_live)
 
     carried = (rotated, running_max, running_sum, accumulated)
-    every_pair = lax.all_gather(packed, "ctx", axis=2, tiled=True)
+    every_pair = pass_along(packed, "ctx", 2)
     every_transfer, every_doc = (
         lax.all_gather(transfer[None].astype(jnp.bfloat16), "ctx", axis=0, tiled=True).astype(
             jnp.float32

time: 905 us -> 1060 us (1.17)
  waiting for transfers between devices: 223 us -> 300 us
  blocking collectives: 28.1 us -> 60.9 us
  local copies, waits for them, and re-layouts: 52.5 us -> 81.2 us
    ppermute x0 -> x7, waiting for transfers between devices: none -> 259 us  [pass_along(): lax.ppermute(held, mesh_axis, [(i, (i + 1) % devices) for i in range(devi...]
    all_gather x1 -> x0, waiting for transfers between devices: 180 us -> none  [on_device(): every_pair = lax.all_gather(packed, 'ctx', axis=2, tiled=True)]
    all_gather x1, blocking collectives: 28.1 us -> 60.9 us  [on_device(): lax.all_gather(doc_float.astype(jnp.bfloat16), 'ctx', axis=0, tiled=True)]
    unnamed x58 -> x82, local copies, waits for them, and re-layouts: 13.8 us -> 35.6 us
  transfers between devices with their start and end apart: 3 -> 9, of which waited for: 2 -> 6; matrix products, arithmetic and copies ran while one was open for 8% -> 6% of each run, Pallas kernels for 0% -> 0%
where the time goes in v1:
time: 1060 us; the launch traced here: 1050 us
  other arithmetic  342 us (32%)
  waiting for transfers between devices  300 us (28%)
  matrix products  244 us (23%)
  local copies, waits for them, and re-layouts  81.2 us (8%)
  blocking collectives  60.9 us (6%)
  between operations  14.5 us (1%)
    another operation x3, other arithmetic, shard_operators(): lax.linalg.triangular_solve(unit_lower, jnp.concatenate([key_proj, vector...  316 us
    ppermute x7, waiting for transfers between devices, pass_along(): lax.ppermute(held, mesh_axis, [(i, (i + 1) % devices) for i in range(devi...  259 us
    all_gather x1, blocking collectives, on_device(): lax.all_gather(doc_float.astype(jnp.bfloat16), 'ctx', axis=0, tiled=True)  60.9 us
    dot_general x7, matrix products, attend(): jnp.einsum('hqk,hkd->hqd', weights.astype(jnp.bfloat16), key_pair[1], pre...  59.1 us
    another operation x7, matrix products, shard_operators(): lax.linalg.triangular_solve(unit_lower, jnp.concatenate([key_proj, vector...  51.7 us
    reduce_scatter x1, waiting for transfers between devices, on_device(): lax.psum_scatter(jnp.dot(token_rows, out_weight, preferred_element_type=j...  41.1 us
    unnamed x82, local copies, waits for them, and re-layouts  35.6 us
    dot_general x7, matrix products, attend(): turned = jnp.einsum('hqd,hde->hqe', turned, transfer_in, precision=highest)  23.7 us
  transfers between devices with their start and end apart: 9, of which 6 were waited for; matrix products, arithmetic and copies ran while one was open for 6% of the time, Pallas kernels for 0%

profile of v1, /device:TPU:0, one launch (start us, length us, event | category | flops | bytes accessed | tf_op | source)
XLA Modules:
  0.0 1046.7 jit_solution(1194075280461022786)
XLA Ops:
  16.1 6.1 broadcast_select_fusion
  22.2 11.6 %select_add_fusion = f32[8,512,512]{1,2,0:T(8,128)} fusion(f32[512,512]{0,1:T(8,128)S(1)} %copy-done.27, f32[512,512]{0,1:T(8,128)S(1)} %copy-done.26, f32[8,512]{1,0:T(8,128)S(1)} %multiply_bitcast_fusion, pred[512,512]{0,1:T(8,128)(4,1)S(1)} %get-tuple-element.265, pred[512,512]{0,1:T(8,128)(4,1)S(1)} %copy-done.28, ...), kind=kOutput, calls=%fused_computation.42 | convolution fusion | flops 3231711232 | bytes 13123584 | tf_op jit(solution)/shard_map/vmap()/dot_general | solution.py:27
  33.8 17.5 %while.21 = (s32[]{:T(128)}, f32[8,512,512]{1,2,0:T(8,128)}, s32[4,2]{0,1:T(2,128)S(1)}, f32[4,8,128,128]{3,2,0,1:T(8,128)}, s32[]{:T(128)}) while((s32[]{:T(128)}, f32[8,512,512]{1,2,0:T(8,128)}, s32[4,2]{0,1:T(2,128)S(1)}, f32[4,8,128,128]{3,2,0,1:T(8,128)}, s32[]{:T(128)}) %tuple.58), condition=%wide.while_cond, body=%wide.while_body.sunk | while | flops 2 | bytes 3145845 | solution.py:32
  51.2 316.0 %custom-call.3 = f32[8,4,128,128]{2,3,1,0:T(8,128)} custom-call(f32[8,4,128,128]{3,2,1,0:T(8,128)} %bitcast.134), custom_call_target="InvertDiagBlocksLowerTriangular" | custom-call | tf_op jit(solution)/shard_map/vmap()/triangular_solve | solution.py:32
  367.3 4.7 fusion.52
  372.0 6.0 fusion.90
  378.0 4.8 fusion.56
  382.8 11.0 %fusion.33 = f32[8,128,640]{1,2,0:T(8,128)S(1)} fusion(f32[8,128,640]{2,1,0:T(8,128)S(1)} %fusion.56, f32[8,128,640]{2,1,0:T(8,128)S(1)} %fusion.52, f32[8,512,512]{1,2,0:T(8,128)} %get-tuple-element.437), kind=kOutput, calls=%fused_computation.54 | convolution fusion | flops 2014576640 | bytes 8912896 | tf_op jit(solution)/shard_map/vmap()/triangular_solve | solution.py:32
  393.9 3.0 fusion.49
  398.4 15.7 %fusion.21 = f32[8,128,640]{1,2,0:T(8,128)} fusion(f32[8,128,640]{2,1,0:T(8,128)S(1)} %fusion.49, f32[8,128,640]{2,1,0:T(8,128)S(1)} %fusion.56, f32[8,128,640]{2,1,0:T(8,128)S(1)} %fusion.52, f32[8,512,512]{1,2,0:T(8,128)} %get-tuple-element.437), kind=kOutput, calls=%fused_computation.43 | convolution fusion | flops 3023831040 | bytes 12058624 | tf_op jit(solution)/shard_map/vmap()/triangular_solve | solution.py:32
  414.1 3.2 copy.108
  417.3 3.3 copy.107
  420.6 3.2 copy.106
  423.8 6.5 fusion.59
  433.3 10.1 fusion.70
  443.6 3.0 collective-permute-start
  446.6 48.7 %collective-permute-done = bf16[2,8,512,128]{3,2,1,0:T(8,128)(2,1)S(1)} collective-permute-done((bf16[2,8,512,128]{3,2,1,0:T(8,128)(2,1)S(1)}, bf16[2,8,512,128]{3,2,1,0:T(8,128)(2,1)S(1)}, u32[]{:S(2)}, u32[]{:S(2)}) %collective-permute-start) | collective-permute-done | bytes 2097184 | tf_op jit(solution)/shard_map/ppermute | solution.py:15
  495.3 49.5 %collective-permute-done.1 = bf16[2,8,512,128]{3,2,1,0:T(8,128)(2,1)S(1)} collective-permute-done((bf16[2,8,512,128]{3,2,1,0:T(8,128)(2,1)S(1)}, bf16[2,8,512,128]{3,2,1,0:T(8,128)(2,1)S(1)}, u32[]{:S(2)}, u32[]{:S(2)}) %collective-permute-start.1) | collective-permute-done | bytes 2097184 | tf_op jit(solution)/shard_map/ppermute | solution.py:15
  546.1 48.6 %collective-permute-done.2 = bf16[2,8,512,128]{3,2,1,0:T(8,128)(2,1)S(1)} collective-permute-done((bf16[2,8,512,128]{3,2,1,0:T(8,128)(2,1)S(1)}, bf16[2,8,512,128]{3,2,1,0:T(8,128)(2,1)S(1)}, u32[]{:S(2)}, u32[]{:S(2)}) %collective-permute-start.2) | collective-permute-done | bytes 2097184 | tf_op jit(solution)/shard_map/ppermute | solution.py:15
  596.0 47.8 %collective-permute-done.3 = bf16[2,8,512,128]{3,2,1,0:T(8,128)(2,1)} collective-permute-done((bf16[2,8,512,128]{3,2,1,0:T(8,128)(2,1)S(1)}, bf16[2,8,512,128]{3,2,1,0:T(8,128)(2,1)}, u32[]{:S(2)}, u32[]{:S(2)}) %collective-permute-start.3) | collective-permute-done | bytes 2097184 | tf_op jit(solution)/shard_map/ppermute | solution.py:15
  645.4 2.9 fusion.76
  653.0 64.8 %collective-permute-done.4 = bf16[2,8,512,128]{3,2,1,0:T(8,128)(2,1)} collective-permute-done((bf16[2,8,512,128]{3,2,1,0:T(8,128)(2,1)}, bf16[2,8,512,128]{3,2,1,0:T(8,128)(2,1)}, u32[]{:S(2)}, u32[]{:S(2)}) %collective-permute-start.4) | collective-permute-done | bytes 2097184 | tf_op jit(solution)/shard_map/ppermute | solution.py:15
  718.2 4.8 fusion.84
  723.1 3.3 copy-done.3
  726.3 15.8 %convert_subtract_fusion = f32[8,512,128]{2,1,0:T(8,128)} fusion(f32[8,512,128]{1,2,0:T(8,128)S(1)} %copy-done.7, f32[8,512,512]{2,1,0:T(8,128)S(1)} %fusion.84, f32[8,512]{1,0:T(8,128)S(1)} %multiply_bitcast_fusion, pred[512,512]{0,1:T(8,128)(4,1)S(1)} %iota_compare_fusion.4, bf16[512,8,128]{2,0,1:T(8,128)(2,1)S(1)} %copy-done.8), kind=kOutput, calls=%fused_computation.88 | convolution fusion | flops 3226468352 | bytes 13910016 | tf_op jit(solution)/shard_map/vmap()/dot_general | solution.py:51
  744.1 20.2 %fusion.29 = f32[8,512,512]{1,2,0:T(8,128)} fusion(f32[8,512,512]{2,1,0:T(8,128)} %copy-done.3, f32[8,512]{1,0:T(8,128)S(1)} %multiply_bitcast_fusion, pred[512,512]{0,1:T(8,128)(4,1)S(1)} %iota_compare_fusion.4, f32[8,128,640]{1,2,0:T(8,128)} %fusion.59, f32[8,128,640]{1,2,0:T(8,128)} %copy.108, f32[8,128,640]{1,2,0:T(8,128)} %copy.107, ...), kind=kOutput, calls=%fused_computation.51 | convolution fusion | flops 12895387648 | bytes 27541504 | tf_op jit(solution)/shard_map/vmap()/dot_general | solution.py:48
  764.3 60.9 %all-gather.1 = bf16[8,1,512]{2,1,0:T(2,128)(2,1)S(1)} all-gather(bf16[1,1,512]{2,1,0:T(2,128)(2,1)S(1)} %reshape.148), channel_id=1, replica_groups=mesh['ctx'=8,'head'=4] {'ctx'}, dimensions={0}, use_global_device_ids=true | all-gather | bytes 9216 | tf_op jit(solution)/shard_map/all_gather | solution.py:127
  825.5 5.9 fusion.105
  832.6 3.1 fusion.37
  835.7 4.1 convert.4
  861.2 6.9 constant_dynamic-slice_fusion.2
  868.1 118.4 %while.20 = (s32[]{:T(128)}, f32[8,512,128]{1,2,0:T(8,128)S(1)}, f32[8,512]{1,0:T(8,128)S(1)}, f32[8,512]{1,0:T(8,128)S(1)}, f32[8,512,128]{2,1,0:T(8,128)}, /*i...) while((s32[]{:T(128)}, f32[8,512,128]{1,2,0:T(8,128)S(1)}, ...), condition=%wide.region_6.7_spmd, body=%wide.region_3.6_spmd.sunk | while | flops 1904222208 | bytes 77340952 | solution.py:139
  871.4 3.4 convolution_bitcast_fusion.2
  876.6 8.4 multiply_add_fusion.5
  888.3 3.4 convolution_bitcast_fusion.2
  893.5 8.4 multiply_add_fusion.5
  905.2 3.4 convolution_bitcast_fusion.2
  910.4 8.4 multiply_add_fusion.5
  922.1 3.4 convolution_bitcast_fusion.2
  927.3 8.4 multiply_add_fusion.5
  939.1 3.4 convolution_bitcast_fusion.2
  944.3 8.4 multiply_add_fusion.5
  956.0 3.4 convolution_bitcast_fusion.2
  961.2 8.4 multiply_add_fusion.5
  972.9 3.4 convolution_bitcast_fusion.2
  978.1 8.4 multiply_add_fusion.5
  988.8 9.5 convolution_convert_fusion
  998.3 41.1 %reduce-scatter.2.cloned.1.call-done = bf16[128,4096]{1,0:T(8,128)(2,1)} async-done(((bf16[512,4096]{1,0:T(8,128)(2,1)}), bf16[128,4096]{1,0:T(8,128)(2,1)}) %reduce-scatter.2.cloned.1.call-update) | async-done | bytes 1048592 | tf_op jit(solution)/shard_map/reduce_scatter | solution.py:142
  (212 shorter events, 102.7 us)
Async XLA Ops:
  6.5 2.6 copy-start.23
  6.5 829.2 %all-gather.4.cloned.1.call-start = ((), (), s32[]{:S(2)}) async-start(), calls=%async_computation.2 | async-start | bytes 2359296 | tf_op jit(solution)/shard_map/all_gather | solution.py:124
  9.7 1.4 copy-start.5
  11.0 2.0 copy-start.24
  13.0 3.0 copy-start.29
  16.0 6.2 copy-start.15
  16.0 6.2 copy-start.26
  16.0 6.2 copy-start.27
  16.1 6.1 copy-start.28
  367.3 10.7 %copy-start.22 = (f32[8,4,128,128]{2,3,1,0:T(8,128)S(1)}, f32[8,4,128,128]{2,3,1,0:T(8,128)}, u32[]{:S(2)}) copy-start(f32[8,4,128,128]{2,3,1,0:T(8,128)} %custom-call.3) | copy-start | bytes 6291460
  372.0 24.8 %copy-start.1 = (f32[8,128,640]{2,1,0:T(8,128)}, f32[8,128,640]{2,1,0:T(8,128)S(1)}, u32[]{:S(2)}) copy-start(f32[8,128,640]{2,1,0:T(8,128)S(1)} %fusion.52) | copy-start | bytes 7864324
  372.0 21.8 %slice-start = ((s8[8388608]{0:T(1024)(128)(4,1)}), s8[4194304]{0:T(1024)(128)(4,1)S(1)}, s32[]{:S(2)}) async-start(s8[8388608]{0:T(1024)(128)(4,1)} %bitcast.123), calls=%async_computation.3 | async-start | bytes 8388608
  378.0 15.8 %slice-start.1 = ((s8[8388608]{0:T(1024)(128)(4,1)}), s8[4194304]{0:T(1024)(128)(4,1)S(1)}, s32[]{:S(2)}) async-start(s8[8388608]{0:T(1024)(128)(4,1)} %bitcast.123), calls=%async_computation.4 | async-start | bytes 8388608
  382.8 14.1 %copy-start.2 = (f32[8,128,640]{2,1,0:T(8,128)}, f32[8,128,640]{2,1,0:T(8,128)S(1)}, u32[]{:S(2)}) copy-start(f32[8,128,640]{2,1,0:T(8,128)S(1)} %fusion.56) | copy-start | bytes 7864324
  396.9 1.5 copy-start.4
  423.8 6.5 copy-start.25
  433.3 210.5 %copy-start.10 = (f32[8,128,640]{1,2,0:T(8,128)S(1)}, f32[8,128,640]{1,2,0:T(8,128)}, u32[]{:S(2)}) copy-start(f32[8,128,640]{1,2,0:T(8,128)} %copy.108) | copy-start | bytes 7864324
  433.3 210.5 %copy-start.11 = (f32[8,128,640]{1,2,0:T(8,128)S(1)}, f32[8,128,640]{1,2,0:T(8,128)}, u32[]{:S(2)}) copy-start(f32[8,128,640]{1,2,0:T(8,128)} %copy.107) | copy-start | bytes 7864324
  433.3 210.5 %copy-start.12 = (f32[8,128,640]{1,2,0:T(8,128)S(1)}, f32[8,128,640]{1,2,0:T(8,128)}, u32[]{:S(2)}) copy-start(f32[8,128,640]{1,2,0:T(8,128)} %copy.106) | copy-start | bytes 7864324
  443.4 200.6 %copy-start.13 = (bf16[1,8,512,128]{3,2,1,0:T(8,128)(2,1)}, bf16[1,8,512,128]{3,2,1,0:T(8,128)(2,1)S(1)}, u32[]{:S(2)}) copy-start(bf16[1,8,512,128]{3,2,1,0:T(8,128)(2,1)S(1)} %fusion.70) | copy-start | bytes 3145732
  443.4 200.4 %copy-start.9 = (f32[8,128,640]{1,2,0:T(8,128)S(1)}, f32[8,128,640]{1,2,0:T(8,128)}, u32[]{:S(2)}) copy-start(f32[8,128,640]{1,2,0:T(8,128)} %fusion.59) | copy-start | bytes 7864324
  443.6 51.7 %collective-permute-start = (bf16[2,8,512,128]{3,2,1,0:T(8,128)(2,1)S(1)}, bf16[2,8,512,128]{3,2,1,0:T(8,128)(2,1)S(1)}, u32[]{:S(2)}, u32[]{:S(2)}) collective-permute-start(bf16[2,8,512,128]{3,2,1,0:T(8,128)(2,1)S(1)} %pad_maximum_fusion.7), channel_id=1, source_target_pairs={{0,4},{4,8},{8,12},{12,16},{16,20},{20,24},{24,28},{28,0},{1,5},{5... | collective-permute-start | bytes 6291464 | tf_op jit(solution)/shard_map/ppermute | solution.py:15
  495.3 148.7 %copy-start.16 = (bf16[2,8,512,128]{3,2,1,0:T(8,128)(2,1)}, bf16[2,8,512,128]{3,2,1,0:T(8,128)(2,1)S(1)}, u32[]{:S(2)}) copy-start(bf16[2,8,512,128]{3,2,1,0:T(8,128)(2,1)S(1)} %collective-permute-done) | copy-start | bytes 6291460
  495.3 49.5 %collective-permute-start.1 = (bf16[2,8,512,128]{3,2,1,0:T(8,128)(2,1)S(1)}, bf16[2,8,512,128]{3,2,1,0:T(8,128)(2,1)S(1)}, u32[]{:S(2)}, u32[]{:S(2)}) collective-permute-start(bf16[2,8,512,128]{3,2,1,0:T(8,128)(2,1)S(1)} %collective-permute-done), channel_id=1, source_target_pairs={{0,4},{4,8},{8,12},{12,16},{16,20},{20,24},{24,28},{28,0},{1,5},{5... | collective-permute-start | bytes 6291464 | tf_op jit(solution)/shard_map/ppermute | solution.py:15
  544.8 1.3 copy-start.18
  546.1 48.6 %collective-permute-start.2 = (bf16[2,8,512,128]{3,2,1,0:T(8,128)(2,1)S(1)}, bf16[2,8,512,128]{3,2,1,0:T(8,128)(2,1)S(1)}, u32[]{:S(2)}, u32[]{:S(2)}) collective-permute-start(bf16[2,8,512,128]{3,2,1,0:T(8,128)(2,1)S(1)} %collective-permute-done.1), channel_id=1, source_target_pairs={{0,4},{4,8},{8,12},{12,16},{16,20},{20,24},{24,28},{28,0},{1,5},{5... | collective-permute-start | bytes 6291464 | tf_op jit(solution)/shard_map/ppermute | solution.py:15
  594.7 1.3 copy-start.20
  596.0 47.8 %collective-permute-start.3 = (bf16[2,8,512,128]{3,2,1,0:T(8,128)(2,1)S(1)}, bf16[2,8,512,128]{3,2,1,0:T(8,128)(2,1)}, u32[]{:S(2)}, u32[]{:S(2)}) collective-permute-start(bf16[2,8,512,128]{3,2,1,0:T(8,128)(2,1)S(1)} %collective-permute-done.2), channel_id=1, source_target_pairs={{0,4},{4,8},{8,12},{12,16},{16,20},{20,24},{24,28},{28,0},{1,5},{5... | collective-permute-start | bytes 6291464 | tf_op jit(solution)/shard_map/ppermute | solution.py:15
  643.8 74.0 %collective-permute-start.4 = (bf16[2,8,512,128]{3,2,1,0:T(8,128)(2,1)}, bf16[2,8,512,128]{3,2,1,0:T(8,128)(2,1)}, u32[]{:S(2)}, u32[]{:S(2)}) collective-permute-start(bf16[2,8,512,128]{3,2,1,0:T(8,128)(2,1)} %collective-permute-done.3), channel_id=1, source_target_pairs={{0,4},{4,8},{8,12},{12,16},{16,20},{20,24},{24,28},{28,0},{1,5},{5... | collective-permute-start | bytes 6291464 | tf_op jit(solution)/shard_map/ppermute | solution.py:15
  644.0 1.4 copy-start.6
  648.3 391.1 %reduce-scatter.2.cloned.1.call-start = ((), (), s32[]{:S(2)}) async-start(), calls=%async_computation.1 | async-start | bytes 5242880 | tf_op jit(solution)/shard_map/reduce_scatter | solution.py:142
  653.0 73.4 %copy-start.7 = (f32[8,512,128]{1,2,0:T(8,128)S(1)}, f32[8,512,128]{1,2,0:T(8,128)}, u32[]{:S(2)}) copy-start(f32[8,512,128]{1,2,0:T(8,128)} %copy-done.6) | copy-start | bytes 6291460
  653.0 73.4 %copy-start.8 = (bf16[512,8,128]{2,0,1:T(8,128)(2,1)S(1)}, bf16[512,8,128]{2,0,1:T(8,128)(2,1)}, u32[]{:S(2)}) copy-start(bf16[512,8,128]{2,0,1:T(8,128)(2,1)} %copy.81) | copy-start | bytes 3145732
  717.8 46.5 %collective-permute-start.5 = (bf16[2,8,512,128]{3,2,1,0:T(8,128)(2,1)}, bf16[2,8,512,128]{3,2,1,0:T(8,128)(2,1)}, u32[]{:S(2)}, u32[]{:S(2)}) collective-permute-start(bf16[2,8,512,128]{3,2,1,0:T(8,128)(2,1)} %collective-permute-done.4), channel_id=1, source_target_pairs={{0,4},{4,8},{8,12},{12,16},{16,20},{20,24},{24,28},{28,0},{1,5},{5... | collective-permute-start | bytes 6291464 | tf_op jit(solution)/shard_map/ppermute | solution.py:15
  723.0 3.3 copy-start.3
  744.1 20.2 %copy-start.30 = (s32[512]{0:T(512)S(1)}, s32[512]{0:T(512)}, u32[]{:S(2)}) copy-start(s32[512]{0:T(512)} %param.14) | copy-start | bytes 6148
  764.3 75.5 %collective-permute-start.6 = (bf16[2,8,512,128]{3,2,1,0:T(8,128)(2,1)}, bf16[2,8,512,128]{3,2,1,0:T(8,128)(2,1)}, u32[]{:S(2)}, u32[]{:S(2)}) collective-permute-start(bf16[2,8,512,128]{3,2,1,0:T(8,128)(2,1)} %collective-permute-done.5), channel_id=1, source_target_pairs={{0,4},{4,8},{8,12},{12,16},{16,20},{20,24},{24,28},{28,0},{1,5},{5... | collective-permute-start | bytes 6291464 | tf_op jit(solution)/shard_map/ppermute | solution.py:15
  845.4 2.2 copy-start.21
  847.7 1.6 copy-start.19
  849.2 1.6 copy-start.17
  850.8 1.2 copy-start.14
  871.4 5.2 copy-start
  888.3 5.2 copy-start
  905.2 5.2 copy-start
  922.1 5.2 copy-start
  939.0 5.2 copy-start
  956.0 5.2 copy-start
  972.9 5.2 copy-start
Sparse Core Ops, SparseCore 0:
  648.4 66.3 all-gather.3
  998.4 40.9 reduce-scatter.1
